TPU v7x, 256 devices: a whole 4x4x8 slice. The times are simulated.
256 devices in a mesh: sec: 16 (over x, y), vel: 16 (over z, core).
Axes of the slice: x: 4, y: 4, z: 8, core: 2. Of those that a mesh axis runs over, the one named last changes fastest.
Arguments:
- distribution: float32 [13824, 4096], P('vel', 'sec'), may hold values from -6 to 6
- collision: float32 [4096], P('sec'), may hold values from 0.05 to 2
- lower_blocks: float32 [25, 4096], P(None, 'sec'), may hold values from -0.6 to 0.6
- upper_blocks: float32 [25, 4096], P(None, 'sec'), may hold values from -0.6 to 0.6
- diag_inverse: float32 [25, 4096], P(None, 'sec'), may hold values from -0.2 to 1.4
Outputs:
- new_distribution: float32 [13824, 4096], P('vel', 'sec')
- macro: float32 [5, 4096], P(None, 'sec')
All inputs are finite; a program needn't handle non-finite values.
Results may differ from a plain program's by a relative error of at most 0.0003.
Values sent between devices are 32-bit elements; how exact they have to be, the bound alone decides.
No kernel may reach another device: no remote copies, remote signals or barrier semaphores. Data moves between devices by JAX's collectives and lax.ppermute only.
A program may use at most 64 MiB of HBM per device.

v0:
```python
import math
import jax
import jax.numpy as jnp
import numpy as np
from jax import lax
from jax.sharding import PartitionSpec as P

NXI = 24
TUBES = 128
JACOBI = 4
NEWTON = 2
HIGH = lax.Precision.HIGHEST
pseudo_rate = 1.0


def passed_along(block, axis, distance):
    devices = range(lax.axis_size(axis))
    route = [(i - distance, i) for i in devices if i - distance in devices]
    return lax.ppermute(block, axis, route)


def extended(array, sides, width):
    for axis, dim in sides:
        count, length = (lax.axis_size(axis), array.shape[dim])
        up = [(i, (i + 1) % count) for i in range(count - 1)]
        down = [(j, i) for i, j in up]
        last = lax.slice_in_dim(array, length - width, length, axis=dim)
        first = lax.slice_in_dim(array, 0, width, axis=dim)
        before = lax.ppermute(last, axis, up)
        after = lax.ppermute(first, axis, down)
        array = jnp.concatenate([before, array, after], axis=dim)
    return array


def hermite_rule(count):
    quarter = math.pi ** (-0.25)
    found = []
    last_slope = 1.0
    for index in range(count // 2):
        if index == 0:
            guess = math.sqrt(2.0 * count + 1.0) - 1.85575 * (2.0 * count + 1.0) ** (-0.16667)
        elif index == 1:
            guess = guess - 1.14 * count**0.426 / guess
        elif index == 2:
            guess = 1.86 * guess - 0.86 * found[0][0]
        elif index == 3:
            guess = 1.91 * guess - 0.91 * found[1][0]
        else:
            guess = 2.0 * guess - found[index - 2][0]
        for repeat in range(60):
            current = quarter
            previous = 0.0
            for order in range(count):
                older = previous
                previous = current
                current = (
                    guess * math.sqrt(2.0 / (order + 1)) * previous
                    - math.sqrt(order / (order + 1.0)) * older
                )
            last_slope = math.sqrt(2.0 * count) * previous
            guess = guess - current / last_slope
        found.append((guess, 2.0 / (last_slope * last_slope)))
    positive = found[::-1]
    points = [-pair[0] for pair in found] + [pair[0] for pair in positive]
    weights = [pair[1] for pair in found] + [pair[1] for pair in positive]
    return (np.array(points), np.array(weights))


def node_tables(axis_points):
    points, weights = hermite_rule(axis_points)
    node_index = np.arange(axis_points**3)
    idx_x = node_index % axis_points
    idx_z = node_index // axis_points % axis_points
    idx_y = node_index // (axis_points * axis_points)
    along_x = points[idx_x]
    along_y = points[idx_y]
    along_z = points[idx_z]
    node_weight = weights[idx_x] * weights[idx_y] * weights[idx_z] / math.pi**1.5
    energy = along_x**2 + along_y**2 + along_z**2 - 1.5
    moment_basis = np.stack([along_x * 0.0 + 1.0, along_x, along_y, along_z, energy])
    norm_scale = np.array([1.0, 0.5, 0.5, 0.5, 1.5])
    return (
        along_x,
        node_weight,
        moment_basis * node_weight[None, :],
        moment_basis / norm_scale[:, None],
    )


def apply_block(matrices, vector):
    shaped = matrices.reshape((5, 5) + vector.shape[1:])
    return jnp.sum(shaped * vector[None], axis=1)


def affine_combine(earlier_map, later_map):
    return (later_map[0] * earlier_map[0], later_map[0] * earlier_map[1] + later_map[1])


def newton_sums(loaded, signed, shift_mass, shift_flow):
    growth = jnp.exp(shift_mass + shift_flow * signed)
    scaled = loaded * growth
    excess = loaded * (growth - 1.0)
    return jnp.stack(
        [
            jnp.sum(scaled),
            jnp.sum(scaled * signed),
            jnp.sum(scaled * signed * signed),
            jnp.sum(excess),
            jnp.sum(excess * signed),
        ]
    )


def newton_update(shift_mass, shift_flow, sums, goal_mass, goal_flow):
    resid_mass = sums[3] - goal_mass
    resid_flow = sums[4] - goal_flow
    determinant = sums[0] * sums[2] - sums[1] * sums[1]
    new_mass = shift_mass - (sums[2] * resid_mass - sums[1] * resid_flow) / determinant
    new_flow = shift_flow - (sums[0] * resid_flow - sums[1] * resid_mass) / determinant
    return (new_mass, new_flow)


def body(distribution, collision, lower_blocks, upper_blocks, diag_inverse):
    node_count = distribution.shape[0]
    cell_count = distribution.shape[1]
    length = cell_count // TUBES
    node_rows = node_count // NXI
    half_nodes = NXI // 2
    along_x, node_weight, weighted_np, rebuild_np = node_tables(NXI)
    all_signed = jnp.asarray(along_x, jnp.float32)
    all_mass = jnp.asarray(node_weight, jnp.float32)
    offset = lax.axis_index("vel") * node_count
    weighted = lax.dynamic_slice_in_dim(
        jnp.asarray(weighted_np, jnp.float32), offset, node_count, 1
    )
    rebuild = lax.dynamic_slice_in_dim(jnp.asarray(rebuild_np, jnp.float32), offset, node_count, 1)
    signed = lax.dynamic_slice_in_dim(all_signed, offset, node_count, 0)
    node_mass = lax.dynamic_slice_in_dim(all_mass, offset, node_count, 0)
    old_moments = lax.psum(jnp.dot(weighted, distribution, precision=HIGH), "vel")
    target = jnp.dot(rebuild.T, old_moments, precision=HIGH)
    total_length = length * lax.axis_size("sec")
    thickness = collision.reshape(1, 1, length, TUBES)
    node_speed = jnp.abs(signed).reshape(node_rows, NXI, 1, 1)
    denominator = node_speed * total_length + thickness + pseudo_rate
    carry_rate = node_speed * total_length / denominator
    drive_term = (
        thickness * target.reshape(node_rows, NXI, length, TUBES)
        + pseudo_rate * distribution.reshape(node_rows, NXI, length, TUBES)
    ) / denominator
    prod_neg, local_neg = lax.associative_scan(
        affine_combine,
        (carry_rate[:, :half_nodes], drive_term[:, :half_nodes]),
        reverse=True,
        axis=2,
    )
    prod_pos, local_pos = lax.associative_scan(
        affine_combine, (carry_rate[:, half_nodes:], drive_term[:, half_nodes:]), axis=2
    )
    summary_pos = (prod_pos[:, :, -1], local_pos[:, :, -1])
    summary_neg = (prod_neg[:, :, 0], local_neg[:, :, 0])

    def relay(turn_index, inflows):
        out_pos = summary_pos[0] * inflows[0] + summary_pos[1]
        out_neg = summary_neg[0] * inflows[1] + summary_neg[1]
        return (passed_along(out_pos, "sec", 1), passed_along(out_neg, "sec", -1))

    start_flows = (jnp.zeros_like(summary_pos[1]), jnp.zeros_like(summary_neg[1]))
    inflow_pos, inflow_neg = lax.fori_loop(0, lax.axis_size("sec") - 1, relay, start_flows)
    field_neg = local_neg + prod_neg * inflow_neg[:, :, None, :]
    field_pos = local_pos + prod_pos * inflow_pos[:, :, None, :]
    half_field = jnp.concatenate([field_neg, field_pos], axis=1).reshape(node_count, cell_count)
    half_moments = lax.psum(jnp.dot(weighted, half_field, precision=HIGH), "vel")
    residual = (half_moments - old_moments).reshape(5, length, TUBES)
    lower_r = lower_blocks.reshape(25, length, TUBES)
    upper_r = upper_blocks.reshape(25, length, TUBES)
    inverse_r = diag_inverse.reshape(25, length, TUBES)
    correction = apply_block(inverse_r, residual)
    for sweep_index in range(JACOBI):
        padded = extended(correction, (("sec", 1),), 1)
        correction = apply_block(
            inverse_r,
            residual - apply_block(lower_r, padded[:, :-2]) - apply_block(upper_r, padded[:, 2:]),
        )
    correction = correction.reshape(5, cell_count)
    macro = half_moments + correction
    synthetic = half_field + jnp.dot(rebuild.T, correction, precision=HIGH)
    local_totals = jnp.sum(old_moments - macro, axis=1)[0:2]
    magnitude = jnp.sum(jnp.abs(synthetic), axis=1)
    shift_mass = jnp.zeros((), jnp.float32)
    shift_flow = jnp.zeros((), jnp.float32)
    goals = lax.psum(local_totals, "sec")
    loaded = node_mass * magnitude
    for newton_turn in range(NEWTON):
        sums = lax.psum(newton_sums(loaded, signed, shift_mass, shift_flow), ("sec", "vel"))
        shift_mass, shift_flow = newton_update(shift_mass, shift_flow, sums, goals[0], goals[1])
    growth = jnp.exp(shift_mass + shift_flow * signed)
    new_distribution = synthetic + jnp.abs(synthetic) * (growth[:, None] - 1.0)
    return (new_distribution, macro)


def solution(mesh):
    in_specs = (P("vel", "sec"), P("sec"), P(None, "sec"), P(None, "sec"), P(None, "sec"))
    out_specs = (P("vel", "sec"), P(None, "sec"))
    return jax.shard_map(body, mesh=mesh, in_specs=in_specs, out_specs=out_specs, check_vma=False)
```

profile of v0, /device:TPU:1, one launch (start us, length us, event | category | flops | bytes accessed | tf_op | source)
XLA Modules:
  0.0 529.8 jit_solution(13319355678150819827)
XLA Ops:
  3.6 27.9 %psum.35 = f32[5,256]{1,0:T(8,128)S(1)} all-reduce(f32[5,256]{1,0:T(8,128)S(1)} %fusion.12), channel_id=1, replica_groups=mesh['sec'=16,'vel'=16] {'vel'}, use_global_device_ids=true, to_apply=%region_0.0 | all-reduce | flops 1280 | bytes 10240 | tf_op jit(solution)/shard_map/psum | solution.py:139
  44.4 185.1 %while.12 = (s32[]{:T(128)}, f32[36,12,128]{2,1,0:T(8,128)S(1)}, f32[36,12,128]{2,1,0:T(8,128)S(1)}, f32[36,12,128]{2,1,0:T(8,128)S(1)}, f32[36,12,128]{2,1,0:T(...) while((s32[]{:T(128)}, f32[36,12,128]{2,1,0:T(8,128)S(1)}, ...), condition=%wide.region_2.0_spmd, body=%wide.region_1.0_spmd.sunk | while | flops 221186 | bytes 3539109 | solution.py:168
  44.5 3.2 collective-permute-start
  51.3 3.9 collective-permute-done.1
  55.3 3.5 collective-permute-start
  62.4 3.9 collective-permute-done.1
  66.4 4.4 collective-permute-start
  74.5 3.9 collective-permute-done.1
  78.4 4.0 collective-permute-start
  86.1 3.9 collective-permute-done.1
  90.1 4.0 collective-permute-start
  97.7 3.9 collective-permute-done.1
  101.7 3.7 collective-permute-start
  109.1 4.0 collective-permute-done.1
  113.1 3.9 collective-permute-start
  118.5 3.2 collective-permute-done
  121.7 4.2 collective-permute-done.1
  125.9 3.7 collective-permute-start
  131.0 4.3 collective-permute-done
  135.3 4.4 collective-permute-done.1
  139.8 3.7 collective-permute-start
  144.9 5.2 collective-permute-done
  150.1 4.2 collective-permute-done.1
  154.3 3.8 collective-permute-start
  159.6 4.3 collective-permute-done
  163.9 3.9 collective-permute-done.1
  167.8 4.8 collective-permute-start
  174.0 3.7 collective-permute-done
  177.7 3.9 collective-permute-done.1
  181.7 4.3 collective-permute-start
  190.1 3.9 collective-permute-done.1
  194.1 4.3 collective-permute-start
  202.0 3.9 collective-permute-done.1
  206.0 4.0 collective-permute-start
  213.6 3.9 collective-permute-done.1
  217.6 4.3 collective-permute-start
  225.6 3.9 collective-permute-done.1
  232.6 44.9 %psum.36 = f32[5,256]{1,0:T(8,128)S(1)} all-reduce(f32[5,256]{1,0:T(8,128)S(1)} %fusion), channel_id=1, replica_groups=mesh['sec'=16,'vel'=16] {'vel'}, use_global_device_ids=true, to_apply=%region_3.0 | all-reduce | flops 1280 | bytes 10240 | tf_op jit(solution)/shard_map/psum | solution.py:172
  277.7 3.7 collective-permute-start.2
  282.8 3.2 collective-permute-done.3
  286.1 3.7 collective-permute-start.4
  294.3 4.0 collective-permute-start.6
  302.8 4.0 collective-permute-start.8
  314.0 30.6 %psum.38 = f32[2]{0:T(128)S(1)} all-reduce(f32[2]{0:T(128)S(1)} %bitcast.57), channel_id=1, replica_groups=mesh['sec'=16,'vel'=16] {'sec'}, use_global_device_ids=true, to_apply=%region_25.0 | all-reduce | flops 2 | bytes 16 | tf_op jit(solution)/shard_map/psum | solution.py:191
  346.1 3.2 stack.41
  349.9 82.5 %psum.37 = f32[5]{0:T(128)S(1)} all-reduce(f32[5]{0:T(128)S(1)} %stack.41), channel_id=1, replica_groups=mesh['sec'=16,'vel'=16] {'sec','vel'}, use_global_device_ids=true, to_apply=%region_23.0 | all-reduce | flops 5 | bytes 40 | tf_op jit(solution)/shard_map/psum | solution.py:194
  442.2 3.2 stack.47
  445.4 74.4 %psum.39 = f32[5]{0:T(128)S(1)} all-reduce(f32[5]{0:T(128)S(1)} %stack.47), channel_id=1, replica_groups=mesh['sec'=16,'vel'=16] {'sec','vel'}, use_global_device_ids=true, to_apply=%region_31.0 | all-reduce | flops 5 | bytes 40 | tf_op jit(solution)/shard_map/psum | solution.py:194
  (142 shorter events, 87.2 us)
Async XLA Ops:
  0.6 1.7 copy-start
  34.7 0.7 copy-start.6
  44.5 6.9 %collective-permute-start = (f32[36,12,128]{2,1,0:T(8,128)S(1)}, f32[36,12,128]{2,1,0:T(8,128)S(1)}, u32[]{:S(2)}, u32[]{:S(2)}) collective-permute-start(f32[36,12,128]{2,1,0:T(8,128)S(1)} %multiply_add_fusion.6), channel_id=1, source_target_pairs={{0,16},{16,32},{32,48},{48,64},{64,80},{80,96},{96,112},{112,128},... | collective-permute-start | bytes 663560 | tf_op jit(solution)/shard_map/while/body/eval_jaxpr/ppermute | solution.py:19
  47.8 7.5 %collective-permute-start.1 = (f32[36,12,128]{2,1,0:T(8,128)S(1)}, f32[36,12,128]{2,1,0:T(8,128)S(1)}, u32[]{:S(2)}, u32[]{:S(2)}) collective-permute-start(f32[36,12,128]{2,1,0:T(8,128)S(1)} %multiply_add_fusion.7), channel_id=1, source_target_pairs={{16,0},{32,16},{48,32},{64,48},{80,64},{96,80},{112,96},{128,112},... | collective-permute-start | bytes 663560 | tf_op jit(solution)/shard_map/while/body/eval_jaxpr/ppermute | solution.py:19
  55.3 7.1 %collective-permute-start = (f32[36,12,128]{2,1,0:T(8,128)S(1)}, f32[36,12,128]{2,1,0:T(8,128)S(1)}, u32[]{:S(2)}, u32[]{:S(2)}) collective-permute-start(f32[36,12,128]{2,1,0:T(8,128)S(1)} %multiply_add_fusion.6), channel_id=1, source_target_pairs={{0,16},{16,32},{32,48},{48,64},{64,80},{80,96},{96,112},{112,128},... | collective-permute-start | bytes 663560 | tf_op jit(solution)/shard_map/while/body/eval_jaxpr/ppermute | solution.py:19
  58.9 7.5 %collective-permute-start.1 = (f32[36,12,128]{2,1,0:T(8,128)S(1)}, f32[36,12,128]{2,1,0:T(8,128)S(1)}, u32[]{:S(2)}, u32[]{:S(2)}) collective-permute-start(f32[36,12,128]{2,1,0:T(8,128)S(1)} %multiply_add_fusion.7), channel_id=1, source_target_pairs={{16,0},{32,16},{48,32},{64,48},{80,64},{96,80},{112,96},{128,112},... | collective-permute-start | bytes 663560 | tf_op jit(solution)/shard_map/while/body/eval_jaxpr/ppermute | solution.py:19
  66.4 8.1 %collective-permute-start = (f32[36,12,128]{2,1,0:T(8,128)S(1)}, f32[36,12,128]{2,1,0:T(8,128)S(1)}, u32[]{:S(2)}, u32[]{:S(2)}) collective-permute-start(f32[36,12,128]{2,1,0:T(8,128)S(1)} %multiply_add_fusion.6), channel_id=1, source_target_pairs={{0,16},{16,32},{32,48},{48,64},{64,80},{80,96},{96,112},{112,128},... | collective-permute-start | bytes 663560 | tf_op jit(solution)/shard_map/while/body/eval_jaxpr/ppermute | solution.py:19
  70.9 7.5 %collective-permute-start.1 = (f32[36,12,128]{2,1,0:T(8,128)S(1)}, f32[36,12,128]{2,1,0:T(8,128)S(1)}, u32[]{:S(2)}, u32[]{:S(2)}) collective-permute-start(f32[36,12,128]{2,1,0:T(8,128)S(1)} %multiply_add_fusion.7), channel_id=1, source_target_pairs={{16,0},{32,16},{48,32},{64,48},{80,64},{96,80},{112,96},{128,112},... | collective-permute-start | bytes 663560 | tf_op jit(solution)/shard_map/while/body/eval_jaxpr/ppermute | solution.py:19
  78.4 7.7 %collective-permute-start = (f32[36,12,128]{2,1,0:T(8,128)S(1)}, f32[36,12,128]{2,1,0:T(8,128)S(1)}, u32[]{:S(2)}, u32[]{:S(2)}) collective-permute-start(f32[36,12,128]{2,1,0:T(8,128)S(1)} %multiply_add_fusion.6), channel_id=1, source_target_pairs={{0,16},{16,32},{32,48},{48,64},{64,80},{80,96},{96,112},{112,128},... | collective-permute-start | bytes 663560 | tf_op jit(solution)/shard_map/while/body/eval_jaxpr/ppermute | solution.py:19
  82.5 7.5 %collective-permute-start.1 = (f32[36,12,128]{2,1,0:T(8,128)S(1)}, f32[36,12,128]{2,1,0:T(8,128)S(1)}, u32[]{:S(2)}, u32[]{:S(2)}) collective-permute-start(f32[36,12,128]{2,1,0:T(8,128)S(1)} %multiply_add_fusion.7), channel_id=1, source_target_pairs={{16,0},{32,16},{48,32},{64,48},{80,64},{96,80},{112,96},{128,112},... | collective-permute-start | bytes 663560 | tf_op jit(solution)/shard_map/while/body/eval_jaxpr/ppermute | solution.py:19
  90.1 7.7 %collective-permute-start = (f32[36,12,128]{2,1,0:T(8,128)S(1)}, f32[36,12,128]{2,1,0:T(8,128)S(1)}, u32[]{:S(2)}, u32[]{:S(2)}) collective-permute-start(f32[36,12,128]{2,1,0:T(8,128)S(1)} %multiply_add_fusion.6), channel_id=1, source_target_pairs={{0,16},{16,32},{32,48},{48,64},{64,80},{80,96},{96,112},{112,128},... | collective-permute-start | bytes 663560 | tf_op jit(solution)/shard_map/while/body/eval_jaxpr/ppermute | solution.py:19
  94.2 7.5 %collective-permute-start.1 = (f32[36,12,128]{2,1,0:T(8,128)S(1)}, f32[36,12,128]{2,1,0:T(8,128)S(1)}, u32[]{:S(2)}, u32[]{:S(2)}) collective-permute-start(f32[36,12,128]{2,1,0:T(8,128)S(1)} %multiply_add_fusion.7), channel_id=1, source_target_pairs={{16,0},{32,16},{48,32},{64,48},{80,64},{96,80},{112,96},{128,112},... | collective-permute-start | bytes 663560 | tf_op jit(solution)/shard_map/while/body/eval_jaxpr/ppermute | solution.py:19
  101.7 7.4 %collective-permute-start = (f32[36,12,128]{2,1,0:T(8,128)S(1)}, f32[36,12,128]{2,1,0:T(8,128)S(1)}, u32[]{:S(2)}, u32[]{:S(2)}) collective-permute-start(f32[36,12,128]{2,1,0:T(8,128)S(1)} %multiply_add_fusion.6), channel_id=1, source_target_pairs={{0,16},{16,32},{32,48},{48,64},{64,80},{80,96},{96,112},{112,128},... | collective-permute-start | bytes 663560 | tf_op jit(solution)/shard_map/while/body/eval_jaxpr/ppermute | solution.py:19
  105.5 7.6 %collective-permute-start.1 = (f32[36,12,128]{2,1,0:T(8,128)S(1)}, f32[36,12,128]{2,1,0:T(8,128)S(1)}, u32[]{:S(2)}, u32[]{:S(2)}) collective-permute-start(f32[36,12,128]{2,1,0:T(8,128)S(1)} %multiply_add_fusion.7), channel_id=1, source_target_pairs={{16,0},{32,16},{48,32},{64,48},{80,64},{96,80},{112,96},{128,112},... | collective-permute-start | bytes 663560 | tf_op jit(solution)/shard_map/while/body/eval_jaxpr/ppermute | solution.py:19
  113.1 8.5 %collective-permute-start = (f32[36,12,128]{2,1,0:T(8,128)S(1)}, f32[36,12,128]{2,1,0:T(8,128)S(1)}, u32[]{:S(2)}, u32[]{:S(2)}) collective-permute-start(f32[36,12,128]{2,1,0:T(8,128)S(1)} %multiply_add_fusion.6), channel_id=1, source_target_pairs={{0,16},{16,32},{32,48},{48,64},{64,80},{80,96},{96,112},{112,128},... | collective-permute-start | bytes 663560 | tf_op jit(solution)/shard_map/while/body/eval_jaxpr/ppermute | solution.py:19
  117.2 8.7 %collective-permute-start.1 = (f32[36,12,128]{2,1,0:T(8,128)S(1)}, f32[36,12,128]{2,1,0:T(8,128)S(1)}, u32[]{:S(2)}, u32[]{:S(2)}) collective-permute-start(f32[36,12,128]{2,1,0:T(8,128)S(1)} %multiply_add_fusion.7), channel_id=1, source_target_pairs={{16,0},{32,16},{48,32},{64,48},{80,64},{96,80},{112,96},{128,112},... | collective-permute-start | bytes 663560 | tf_op jit(solution)/shard_map/while/body/eval_jaxpr/ppermute | solution.py:19
  125.9 9.4 %collective-permute-start = (f32[36,12,128]{2,1,0:T(8,128)S(1)}, f32[36,12,128]{2,1,0:T(8,128)S(1)}, u32[]{:S(2)}, u32[]{:S(2)}) collective-permute-start(f32[36,12,128]{2,1,0:T(8,128)S(1)} %multiply_add_fusion.6), channel_id=1, source_target_pairs={{0,16},{16,32},{32,48},{48,64},{64,80},{80,96},{96,112},{112,128},... | collective-permute-start | bytes 663560 | tf_op jit(solution)/shard_map/while/body/eval_jaxpr/ppermute | solution.py:19
  129.7 10.1 %collective-permute-start.1 = (f32[36,12,128]{2,1,0:T(8,128)S(1)}, f32[36,12,128]{2,1,0:T(8,128)S(1)}, u32[]{:S(2)}, u32[]{:S(2)}) collective-permute-start(f32[36,12,128]{2,1,0:T(8,128)S(1)} %multiply_add_fusion.7), channel_id=1, source_target_pairs={{16,0},{32,16},{48,32},{64,48},{80,64},{96,80},{112,96},{128,112},... | collective-permute-start | bytes 663560 | tf_op jit(solution)/shard_map/while/body/eval_jaxpr/ppermute | solution.py:19
  139.8 10.2 %collective-permute-start = (f32[36,12,128]{2,1,0:T(8,128)S(1)}, f32[36,12,128]{2,1,0:T(8,128)S(1)}, u32[]{:S(2)}, u32[]{:S(2)}) collective-permute-start(f32[36,12,128]{2,1,0:T(8,128)S(1)} %multiply_add_fusion.6), channel_id=1, source_target_pairs={{0,16},{16,32},{32,48},{48,64},{64,80},{80,96},{96,112},{112,128},... | collective-permute-start | bytes 663560 | tf_op jit(solution)/shard_map/while/body/eval_jaxpr/ppermute | solution.py:19
  143.6 10.7 %collective-permute-start.1 = (f32[36,12,128]{2,1,0:T(8,128)S(1)}, f32[36,12,128]{2,1,0:T(8,128)S(1)}, u32[]{:S(2)}, u32[]{:S(2)}) collective-permute-start(f32[36,12,128]{2,1,0:T(8,128)S(1)} %multiply_add_fusion.7), channel_id=1, source_target_pairs={{16,0},{32,16},{48,32},{64,48},{80,64},{96,80},{112,96},{128,112},... | collective-permute-start | bytes 663560 | tf_op jit(solution)/shard_map/while/body/eval_jaxpr/ppermute | solution.py:19
  154.3 9.5 %collective-permute-start = (f32[36,12,128]{2,1,0:T(8,128)S(1)}, f32[36,12,128]{2,1,0:T(8,128)S(1)}, u32[]{:S(2)}, u32[]{:S(2)}) collective-permute-start(f32[36,12,128]{2,1,0:T(8,128)S(1)} %multiply_add_fusion.6), channel_id=1, source_target_pairs={{0,16},{16,32},{32,48},{48,64},{64,80},{80,96},{96,112},{112,128},... | collective-permute-start | bytes 663560 | tf_op jit(solution)/shard_map/while/body/eval_jaxpr/ppermute | solution.py:19
  158.3 9.5 %collective-permute-start.1 = (f32[36,12,128]{2,1,0:T(8,128)S(1)}, f32[36,12,128]{2,1,0:T(8,128)S(1)}, u32[]{:S(2)}, u32[]{:S(2)}) collective-permute-start(f32[36,12,128]{2,1,0:T(8,128)S(1)} %multiply_add_fusion.7), channel_id=1, source_target_pairs={{16,0},{32,16},{48,32},{64,48},{80,64},{96,80},{112,96},{128,112},... | collective-permute-start | bytes 663560 | tf_op jit(solution)/shard_map/while/body/eval_jaxpr/ppermute | solution.py:19
  167.8 9.9 %collective-permute-start = (f32[36,12,128]{2,1,0:T(8,128)S(1)}, f32[36,12,128]{2,1,0:T(8,128)S(1)}, u32[]{:S(2)}, u32[]{:S(2)}) collective-permute-start(f32[36,12,128]{2,1,0:T(8,128)S(1)} %multiply_add_fusion.6), channel_id=1, source_target_pairs={{0,16},{16,32},{32,48},{48,64},{64,80},{80,96},{96,112},{112,128},... | collective-permute-start | bytes 663560 | tf_op jit(solution)/shard_map/while/body/eval_jaxpr/ppermute | solution.py:19
  172.7 8.9 %collective-permute-start.1 = (f32[36,12,128]{2,1,0:T(8,128)S(1)}, f32[36,12,128]{2,1,0:T(8,128)S(1)}, u32[]{:S(2)}, u32[]{:S(2)}) collective-permute-start(f32[36,12,128]{2,1,0:T(8,128)S(1)} %multiply_add_fusion.7), channel_id=1, source_target_pairs={{16,0},{32,16},{48,32},{64,48},{80,64},{96,80},{112,96},{128,112},... | collective-permute-start | bytes 663560 | tf_op jit(solution)/shard_map/while/body/eval_jaxpr/ppermute | solution.py:19
  181.7 8.4 %collective-permute-start = (f32[36,12,128]{2,1,0:T(8,128)S(1)}, f32[36,12,128]{2,1,0:T(8,128)S(1)}, u32[]{:S(2)}, u32[]{:S(2)}) collective-permute-start(f32[36,12,128]{2,1,0:T(8,128)S(1)} %multiply_add_fusion.6), channel_id=1, source_target_pairs={{0,16},{16,32},{32,48},{48,64},{64,80},{80,96},{96,112},{112,128},... | collective-permute-start | bytes 663560 | tf_op jit(solution)/shard_map/while/body/eval_jaxpr/ppermute | solution.py:19
  186.0 8.0 %collective-permute-start.1 = (f32[36,12,128]{2,1,0:T(8,128)S(1)}, f32[36,12,128]{2,1,0:T(8,128)S(1)}, u32[]{:S(2)}, u32[]{:S(2)}) collective-permute-start(f32[36,12,128]{2,1,0:T(8,128)S(1)} %multiply_add_fusion.7), channel_id=1, source_target_pairs={{16,0},{32,16},{48,32},{64,48},{80,64},{96,80},{112,96},{128,112},... | collective-permute-start | bytes 663560 | tf_op jit(solution)/shard_map/while/body/eval_jaxpr/ppermute | solution.py:19
  194.1 8.0 %collective-permute-start = (f32[36,12,128]{2,1,0:T(8,128)S(1)}, f32[36,12,128]{2,1,0:T(8,128)S(1)}, u32[]{:S(2)}, u32[]{:S(2)}) collective-permute-start(f32[36,12,128]{2,1,0:T(8,128)S(1)} %multiply_add_fusion.6), channel_id=1, source_target_pairs={{0,16},{16,32},{32,48},{48,64},{64,80},{80,96},{96,112},{112,128},... | collective-permute-start | bytes 663560 | tf_op jit(solution)/shard_map/while/body/eval_jaxpr/ppermute | solution.py:19
  198.4 7.5 %collective-permute-start.1 = (f32[36,12,128]{2,1,0:T(8,128)S(1)}, f32[36,12,128]{2,1,0:T(8,128)S(1)}, u32[]{:S(2)}, u32[]{:S(2)}) collective-permute-start(f32[36,12,128]{2,1,0:T(8,128)S(1)} %multiply_add_fusion.7), channel_id=1, source_target_pairs={{16,0},{32,16},{48,32},{64,48},{80,64},{96,80},{112,96},{128,112},... | collective-permute-start | bytes 663560 | tf_op jit(solution)/shard_map/while/body/eval_jaxpr/ppermute | solution.py:19
  206.0 7.7 %collective-permute-start = (f32[36,12,128]{2,1,0:T(8,128)S(1)}, f32[36,12,128]{2,1,0:T(8,128)S(1)}, u32[]{:S(2)}, u32[]{:S(2)}) collective-permute-start(f32[36,12,128]{2,1,0:T(8,128)S(1)} %multiply_add_fusion.6), channel_id=1, source_target_pairs={{0,16},{16,32},{32,48},{48,64},{64,80},{80,96},{96,112},{112,128},... | collective-permute-start | bytes 663560 | tf_op jit(solution)/shard_map/while/body/eval_jaxpr/ppermute | solution.py:19
  210.1 7.5 %collective-permute-start.1 = (f32[36,12,128]{2,1,0:T(8,128)S(1)}, f32[36,12,128]{2,1,0:T(8,128)S(1)}, u32[]{:S(2)}, u32[]{:S(2)}) collective-permute-start(f32[36,12,128]{2,1,0:T(8,128)S(1)} %multiply_add_fusion.7), channel_id=1, source_target_pairs={{16,0},{32,16},{48,32},{64,48},{80,64},{96,80},{112,96},{128,112},... | collective-permute-start | bytes 663560 | tf_op jit(solution)/shard_map/while/body/eval_jaxpr/ppermute | solution.py:19
  217.6 8.0 %collective-permute-start = (f32[36,12,128]{2,1,0:T(8,128)S(1)}, f32[36,12,128]{2,1,0:T(8,128)S(1)}, u32[]{:S(2)}, u32[]{:S(2)}) collective-permute-start(f32[36,12,128]{2,1,0:T(8,128)S(1)} %multiply_add_fusion.6), channel_id=1, source_target_pairs={{0,16},{16,32},{32,48},{48,64},{64,80},{80,96},{96,112},{112,128},... | collective-permute-start | bytes 663560 | tf_op jit(solution)/shard_map/while/body/eval_jaxpr/ppermute | solution.py:19
  222.0 7.5 %collective-permute-start.1 = (f32[36,12,128]{2,1,0:T(8,128)S(1)}, f32[36,12,128]{2,1,0:T(8,128)S(1)}, u32[]{:S(2)}, u32[]{:S(2)}) collective-permute-start(f32[36,12,128]{2,1,0:T(8,128)S(1)} %multiply_add_fusion.7), channel_id=1, source_target_pairs={{16,0},{32,16},{48,32},{64,48},{80,64},{96,80},{112,96},{128,112},... | collective-permute-start | bytes 663560 | tf_op jit(solution)/shard_map/while/body/eval_jaxpr/ppermute | solution.py:19
  229.5 1.0 copy-start.1
  229.5 1.1 copy-start.2
  232.6 45.0 %copy-start.3 = (f32[25,256]{1,0:T(8,128)S(1)}, f32[25,256]{1,0:T(8,128)}, u32[]{:S(2)}) copy-start(f32[25,256]{1,0:T(8,128)} %param.15) | copy-start | bytes 76804
  277.6 5.1 copy-start.4
  277.6 5.1 copy-start.5
  277.7 5.1 collective-permute-start.2
  281.4 4.6 collective-permute-start.3
  286.1 5.1 collective-permute-start.4
  289.9 4.3 collective-permute-start.5
  294.3 5.3 %collective-permute-start.6 = (f32[5,1,128]{2,1,0:T(1,128)S(1)}, f32[5,1,128]{2,1,0:T(1,128)S(1)}, u32[]{:S(2)}, u32[]{:S(2)}) collective-permute-start(f32[5,1,128]{2,1,0:T(1,128)S(1)} %get-tuple-element.91), channel_id=1, source_target_pairs={{0,16},{16,32},{32,48},{48,64},{64,80},{80,96},{96,112},{112,128},... | collective-permute-start | bytes 7688 | tf_op jit(solution)/shard_map/ppermute | solution.py:29
  298.4 4.3 collective-permute-start.7
  302.8 5.3 %collective-permute-start.8 = (f32[5,1,128]{2,1,0:T(1,128)S(1)}, f32[5,1,128]{2,1,0:T(1,128)S(1)}, u32[]{:S(2)}, u32[]{:S(2)}) collective-permute-start(f32[5,1,128]{2,1,0:T(1,128)S(1)} %get-tuple-element.87), channel_id=1, source_target_pairs={{0,16},{16,32},{32,48},{48,64},{64,80},{80,96},{96,112},{112,128},... | collective-permute-start | bytes 7688 | tf_op jit(solution)/shard_map/ppermute | solution.py:29
  306.9 4.3 collective-permute-start.9
where the time goes:
time: 532 us; the launch traced here: 530 us
  blocking collectives  260 us (49%)
  waiting for transfers between devices  116 us (22%)
  starting transfers between devices  100 us (19%)
  between operations  16.2 us (3%)
  local copies, waits for them, and re-layouts  15.9 us (3%)
  other arithmetic  14.6 us (3%)
  matrix products  6.31 us (1%)
    psum x2, blocking collectives, body(): lax.psum(newton_sums(loaded, signed, shift_mass, shift_flow), ('sec', 've...  157 us
    ppermute x30, waiting for transfers between devices, passed_along(): return lax.ppermute(block, axis, route)  104 us
    ppermute x30, starting transfers between devices, passed_along(): return lax.ppermute(block, axis, route)  79.3 us
    psum x1, blocking collectives, body(): lax.psum(jnp.dot(weighted, half_field, precision=HIGH), 'vel')  44.9 us
    psum x1, blocking collectives, body(): goals = lax.psum(local_totals, 'sec')  30.6 us
    psum x1, blocking collectives, body(): lax.psum(jnp.dot(weighted, distribution, precision=HIGH), 'vel')  27.9 us
    ppermute x4, starting transfers between devices, extended(): before = lax.ppermute(last, axis, up)  15.5 us
    ppermute x4, waiting for transfers between devices, extended(): after = lax.ppermute(first, axis, down)  12.3 us
  transfers between devices with their start and end apart: 38, of which 34 were waited for; matrix products, arithmetic and copies ran while one was open for 0% of the time, Pallas kernels for 0%

commit v1 on v0

--- a/solution.py
+++ b/solution.py
@@ -191,7 +191,7 @@
     goals = lax.psum(local_totals, "sec")
     loaded = node_mass * magnitude
     for newton_turn in range(NEWTON):
-        sums = lax.psum(newton_sums(loaded, signed, shift_mass, shift_flow), ("sec", "vel"))
+        sums = lax.psum(lax.psum(newton_sums(loaded, signed, shift_mass, shift_flow), "vel"), "sec")
         shift_mass, shift_flow = newton_update(shift_mass, shift_flow, sums, goals[0], goals[1])
     growth = jnp.exp(shift_mass + shift_flow * signed)
     new_distribution = synthetic + jnp.abs(synthetic) * (growth[:, None] - 1.0)

time: 532 us -> 469 us (0.88); the launches traced: 530 us -> 460 us
  blocking collectives: 260 us -> 190 us
    psum x3 -> x4, blocking collectives: 188 us -> 117 us  [the longest x2 59.1 us: body(): lax.psum(lax.psum(newton_sums(loaded, signed, shift_mass, shift_flow), 'v...]
where the time goes in v1:
time: 469 us; the launch traced here: 460 us
  blocking collectives  190 us (41%)
  waiting for transfers between devices  116 us (25%)
  starting transfers between devices  100 us (21%)
  between operations  16.2 us (3%)
  local copies, waits for them, and re-layouts  16 us (3%)
  other arithmetic  14.6 us (3%)
  matrix products  6.31 us (1%)
    ppermute x30, waiting for transfers between devices, passed_along(): return lax.ppermute(block, axis, route)  104 us
    ppermute x30, starting transfers between devices, passed_along(): return lax.ppermute(block, axis, route)  79.3 us
    psum x2, blocking collectives, body(): lax.psum(lax.psum(newton_sums(loaded, signed, shift_mass, shift_flow), 'v...  59.1 us
    psum x2, blocking collectives, body(): lax.psum(newton_sums(loaded, signed, shift_mass, shift_flow), 'vel')  58.4 us
    psum x1, blocking collectives, body(): lax.psum(jnp.dot(weighted, half_field, precision=HIGH), 'vel')  44.9 us
    psum x1, blocking collectives, body(): lax.psum(jnp.dot(weighted, distribution, precision=HIGH), 'vel')  27.9 us
    ppermute x4, starting transfers between devices, extended(): before = lax.ppermute(last, axis, up)  15.5 us
    ppermute x4, waiting for transfers between devices, extended(): after = lax.ppermute(first, axis, down)  12.3 us
  transfers between devices with their start and end apart: 38, of which 34 were waited for; matrix products, arithmetic and copies ran while one was open for 0% of the time, Pallas kernels for 0%

profile of v1, /device:TPU:1, one launch (start us, length us, event | category | flops | bytes accessed | tf_op | source)
XLA Modules:
  0.0 459.9 jit_solution(16148377514732114357)
XLA Ops:
  3.6 27.9 %psum.49 = f32[5,256]{1,0:T(8,128)S(1)} all-reduce(f32[5,256]{1,0:T(8,128)S(1)} %fusion.12), channel_id=1, replica_groups=mesh['sec'=16,'vel'=16] {'vel'}, use_global_device_ids=true, to_apply=%region_0.0 | all-reduce | flops 1280 | bytes 10240 | tf_op jit(solution)/shard_map/psum | solution.py:139
  44.4 185.1 %while.12 = (s32[]{:T(128)}, f32[36,12,128]{2,1,0:T(8,128)S(1)}, f32[36,12,128]{2,1,0:T(8,128)S(1)}, f32[36,12,128]{2,1,0:T(8,128)S(1)}, f32[36,12,128]{2,1,0:T(...) while((s32[]{:T(128)}, f32[36,12,128]{2,1,0:T(8,128)S(1)}, ...), condition=%wide.region_2.0_spmd, body=%wide.region_1.0_spmd.sunk | while | flops 221186 | bytes 3539109 | solution.py:168
  44.5 3.2 collective-permute-start
  51.3 3.9 collective-permute-done.1
  55.3 3.5 collective-permute-start
  62.4 3.9 collective-permute-done.1
  66.4 4.4 collective-permute-start
  74.5 3.9 collective-permute-done.1
  78.4 4.0 collective-permute-start
  86.1 3.9 collective-permute-done.1
  90.1 4.0 collective-permute-start
  97.7 3.9 collective-permute-done.1
  101.7 3.7 collective-permute-start
  109.1 4.0 collective-permute-done.1
  113.1 3.9 collective-permute-start
  118.5 3.2 collective-permute-done
  121.7 4.2 collective-permute-done.1
  125.9 3.7 collective-permute-start
  131.0 4.3 collective-permute-done
  135.3 4.4 collective-permute-done.1
  139.8 3.7 collective-permute-start
  144.9 5.2 %collective-permute-done = f32[36,12,128]{2,1,0:T(8,128)S(1)} collective-permute-done((f32[36,12,128]{2,1,0:T(8,128)S(1)}, f32[36,12,128]{2,1,0:T(8,128)S(1)}, u32[]{:S(2)}, u32[]{:S(2)}) %collective-permute-start) | collective-permute-done | bytes 221216 | tf_op jit(solution)/shard_map/while/body/eval_jaxpr/ppermute | solution.py:19
  150.1 4.2 collective-permute-done.1
  154.3 3.8 collective-permute-start
  159.6 4.3 collective-permute-done
  163.9 3.9 collective-permute-done.1
  167.8 4.8 %collective-permute-start = (f32[36,12,128]{2,1,0:T(8,128)S(1)}, f32[36,12,128]{2,1,0:T(8,128)S(1)}, u32[]{:S(2)}, u32[]{:S(2)}) collective-permute-start(f32[36,12,128]{2,1,0:T(8,128)S(1)} %multiply_add_fusion.6), channel_id=1, source_target_pairs={{0,16},{16,32},{32,48},{48,64},{64,80},{80,96},{96,112},{112,128},... | collective-permute-start | bytes 663560 | tf_op jit(solution)/shard_map/while/body/eval_jaxpr/ppermute | solution.py:19
  174.0 3.7 collective-permute-done
  177.7 3.9 collective-permute-done.1
  181.7 4.3 collective-permute-start
  190.1 3.9 collective-permute-done.1
  194.1 4.3 collective-permute-start
  202.0 3.9 collective-permute-done.1
  206.0 4.0 collective-permute-start
  213.6 3.9 collective-permute-done.1
  217.6 4.3 collective-permute-start
  225.6 3.9 collective-permute-done.1
  232.6 44.9 %psum.50 = f32[5,256]{1,0:T(8,128)S(1)} all-reduce(f32[5,256]{1,0:T(8,128)S(1)} %fusion), channel_id=1, replica_groups=mesh['sec'=16,'vel'=16] {'vel'}, use_global_device_ids=true, to_apply=%region_3.0 | all-reduce | flops 1280 | bytes 10240 | tf_op jit(solution)/shard_map/psum | solution.py:172
  277.7 3.7 collective-permute-start.2
  282.8 3.2 collective-permute-done.3
  286.1 3.7 collective-permute-start.4
  294.3 4.0 collective-permute-start.6
  302.8 4.0 collective-permute-start.8
  314.8 3.3 stack.41
  318.7 27.9 %psum.51 = f32[5]{0:T(128)S(1)} all-reduce(f32[5]{0:T(128)S(1)} %stack.41), channel_id=1, replica_groups=mesh['sec'=16,'vel'=16] {'vel'}, use_global_device_ids=true, to_apply=%region_23.0 | all-reduce | flops 5 | bytes 40 | tf_op jit(solution)/shard_map/psum | solution.py:194
  346.7 30.6 %all-reduce.8 = (f32[5]{0:T(128)S(1)}, f32[2]{0:T(128)S(1)}) all-reduce(f32[5]{0:T(128)S(1)} %psum.51, f32[2]{0:T(128)S(1)} %bitcast.57), channel_id=1, replica_groups=mesh['sec'=16,'vel'=16] {'sec'}, use_global_device_ids=true, to_apply=%region_24.0 | all-reduce | flops 7 | bytes 56 | tf_op jit(solution)/shard_map/psum | solution.py:194
  390.9 30.4 %psum.54 = f32[5]{0:T(128)S(1)} all-reduce(f32[5]{0:T(128)S(1)} %stack.47), channel_id=1, replica_groups=mesh['sec'=16,'vel'=16] {'vel'}, use_global_device_ids=true, to_apply=%region_32.0 | all-reduce | flops 5 | bytes 40 | tf_op jit(solution)/shard_map/psum | solution.py:194
  421.3 28.5 %psum.55 = f32[5]{0:T(128)S(1)} all-reduce(f32[5]{0:T(128)S(1)} %psum.54), channel_id=1, replica_groups=mesh['sec'=16,'vel'=16] {'sec'}, use_global_device_ids=true, to_apply=%region_33.0 | all-reduce | flops 5 | bytes 40 | tf_op jit(solution)/shard_map/psum | solution.py:194
  (143 shorter events, 90.4 us)
Async XLA Ops:
  0.6 1.7 copy-start
  34.7 0.7 copy-start.6
  44.5 6.9 %collective-permute-start = (f32[36,12,128]{2,1,0:T(8,128)S(1)}, f32[36,12,128]{2,1,0:T(8,128)S(1)}, u32[]{:S(2)}, u32[]{:S(2)}) collective-permute-start(f32[36,12,128]{2,1,0:T(8,128)S(1)} %multiply_add_fusion.6), channel_id=1, source_target_pairs={{0,16},{16,32},{32,48},{48,64},{64,80},{80,96},{96,112},{112,128},... | collective-permute-start | bytes 663560 | tf_op jit(solution)/shard_map/while/body/eval_jaxpr/ppermute | solution.py:19
  47.8 7.5 %collective-permute-start.1 = (f32[36,12,128]{2,1,0:T(8,128)S(1)}, f32[36,12,128]{2,1,0:T(8,128)S(1)}, u32[]{:S(2)}, u32[]{:S(2)}) collective-permute-start(f32[36,12,128]{2,1,0:T(8,128)S(1)} %multiply_add_fusion.7), channel_id=1, source_target_pairs={{16,0},{32,16},{48,32},{64,48},{80,64},{96,80},{112,96},{128,112},... | collective-permute-start | bytes 663560 | tf_op jit(solution)/shard_map/while/body/eval_jaxpr/ppermute | solution.py:19
  55.3 7.1 %collective-permute-start = (f32[36,12,128]{2,1,0:T(8,128)S(1)}, f32[36,12,128]{2,1,0:T(8,128)S(1)}, u32[]{:S(2)}, u32[]{:S(2)}) collective-permute-start(f32[36,12,128]{2,1,0:T(8,128)S(1)} %multiply_add_fusion.6), channel_id=1, source_target_pairs={{0,16},{16,32},{32,48},{48,64},{64,80},{80,96},{96,112},{112,128},... | collective-permute-start | bytes 663560 | tf_op jit(solution)/shard_map/while/body/eval_jaxpr/ppermute | solution.py:19
  58.9 7.5 %collective-permute-start.1 = (f32[36,12,128]{2,1,0:T(8,128)S(1)}, f32[36,12,128]{2,1,0:T(8,128)S(1)}, u32[]{:S(2)}, u32[]{:S(2)}) collective-permute-start(f32[36,12,128]{2,1,0:T(8,128)S(1)} %multiply_add_fusion.7), channel_id=1, source_target_pairs={{16,0},{32,16},{48,32},{64,48},{80,64},{96,80},{112,96},{128,112},... | collective-permute-start | bytes 663560 | tf_op jit(solution)/shard_map/while/body/eval_jaxpr/ppermute | solution.py:19
  66.4 8.1 %collective-permute-start = (f32[36,12,128]{2,1,0:T(8,128)S(1)}, f32[36,12,128]{2,1,0:T(8,128)S(1)}, u32[]{:S(2)}, u32[]{:S(2)}) collective-permute-start(f32[36,12,128]{2,1,0:T(8,128)S(1)} %multiply_add_fusion.6), channel_id=1, source_target_pairs={{0,16},{16,32},{32,48},{48,64},{64,80},{80,96},{96,112},{112,128},... | collective-permute-start | bytes 663560 | tf_op jit(solution)/shard_map/while/body/eval_jaxpr/ppermute | solution.py:19
  70.9 7.5 %collective-permute-start.1 = (f32[36,12,128]{2,1,0:T(8,128)S(1)}, f32[36,12,128]{2,1,0:T(8,128)S(1)}, u32[]{:S(2)}, u32[]{:S(2)}) collective-permute-start(f32[36,12,128]{2,1,0:T(8,128)S(1)} %multiply_add_fusion.7), channel_id=1, source_target_pairs={{16,0},{32,16},{48,32},{64,48},{80,64},{96,80},{112,96},{128,112},... | collective-permute-start | bytes 663560 | tf_op jit(solution)/shard_map/while/body/eval_jaxpr/ppermute | solution.py:19
  78.4 7.7 %collective-permute-start = (f32[36,12,128]{2,1,0:T(8,128)S(1)}, f32[36,12,128]{2,1,0:T(8,128)S(1)}, u32[]{:S(2)}, u32[]{:S(2)}) collective-permute-start(f32[36,12,128]{2,1,0:T(8,128)S(1)} %multiply_add_fusion.6), channel_id=1, source_target_pairs={{0,16},{16,32},{32,48},{48,64},{64,80},{80,96},{96,112},{112,128},... | collective-permute-start | bytes 663560 | tf_op jit(solution)/shard_map/while/body/eval_jaxpr/ppermute | solution.py:19
  82.5 7.5 %collective-permute-start.1 = (f32[36,12,128]{2,1,0:T(8,128)S(1)}, f32[36,12,128]{2,1,0:T(8,128)S(1)}, u32[]{:S(2)}, u32[]{:S(2)}) collective-permute-start(f32[36,12,128]{2,1,0:T(8,128)S(1)} %multiply_add_fusion.7), channel_id=1, source_target_pairs={{16,0},{32,16},{48,32},{64,48},{80,64},{96,80},{112,96},{128,112},... | collective-permute-start | bytes 663560 | tf_op jit(solution)/shard_map/while/body/eval_jaxpr/ppermute | solution.py:19
  90.1 7.7 %collective-permute-start = (f32[36,12,128]{2,1,0:T(8,128)S(1)}, f32[36,12,128]{2,1,0:T(8,128)S(1)}, u32[]{:S(2)}, u32[]{:S(2)}) collective-permute-start(f32[36,12,128]{2,1,0:T(8,128)S(1)} %multiply_add_fusion.6), channel_id=1, source_target_pairs={{0,16},{16,32},{32,48},{48,64},{64,80},{80,96},{96,112},{112,128},... | collective-permute-start | bytes 663560 | tf_op jit(solution)/shard_map/while/body/eval_jaxpr/ppermute | solution.py:19
  94.2 7.5 %collective-permute-start.1 = (f32[36,12,128]{2,1,0:T(8,128)S(1)}, f32[36,12,128]{2,1,0:T(8,128)S(1)}, u32[]{:S(2)}, u32[]{:S(2)}) collective-permute-start(f32[36,12,128]{2,1,0:T(8,128)S(1)} %multiply_add_fusion.7), channel_id=1, source_target_pairs={{16,0},{32,16},{48,32},{64,48},{80,64},{96,80},{112,96},{128,112},... | collective-permute-start | bytes 663560 | tf_op jit(solution)/shard_map/while/body/eval_jaxpr/ppermute | solution.py:19
  101.7 7.4 %collective-permute-start = (f32[36,12,128]{2,1,0:T(8,128)S(1)}, f32[36,12,128]{2,1,0:T(8,128)S(1)}, u32[]{:S(2)}, u32[]{:S(2)}) collective-permute-start(f32[36,12,128]{2,1,0:T(8,128)S(1)} %multiply_add_fusion.6), channel_id=1, source_target_pairs={{0,16},{16,32},{32,48},{48,64},{64,80},{80,96},{96,112},{112,128},... | collective-permute-start | bytes 663560 | tf_op jit(solution)/shard_map/while/body/eval_jaxpr/ppermute | solution.py:19
  105.5 7.6 %collective-permute-start.1 = (f32[36,12,128]{2,1,0:T(8,128)S(1)}, f32[36,12,128]{2,1,0:T(8,128)S(1)}, u32[]{:S(2)}, u32[]{:S(2)}) collective-permute-start(f32[36,12,128]{2,1,0:T(8,128)S(1)} %multiply_add_fusion.7), channel_id=1, source_target_pairs={{16,0},{32,16},{48,32},{64,48},{80,64},{96,80},{112,96},{128,112},... | collective-permute-start | bytes 663560 | tf_op jit(solution)/shard_map/while/body/eval_jaxpr/ppermute | solution.py:19
  113.1 8.5 %collective-permute-start = (f32[36,12,128]{2,1,0:T(8,128)S(1)}, f32[36,12,128]{2,1,0:T(8,128)S(1)}, u32[]{:S(2)}, u32[]{:S(2)}) collective-permute-start(f32[36,12,128]{2,1,0:T(8,128)S(1)} %multiply_add_fusion.6), channel_id=1, source_target_pairs={{0,16},{16,32},{32,48},{48,64},{64,80},{80,96},{96,112},{112,128},... | collective-permute-start | bytes 663560 | tf_op jit(solution)/shard_map/while/body/eval_jaxpr/ppermute | solution.py:19
  117.2 8.7 %collective-permute-start.1 = (f32[36,12,128]{2,1,0:T(8,128)S(1)}, f32[36,12,128]{2,1,0:T(8,128)S(1)}, u32[]{:S(2)}, u32[]{:S(2)}) collective-permute-start(f32[36,12,128]{2,1,0:T(8,128)S(1)} %multiply_add_fusion.7), channel_id=1, source_target_pairs={{16,0},{32,16},{48,32},{64,48},{80,64},{96,80},{112,96},{128,112},... | collective-permute-start | bytes 663560 | tf_op jit(solution)/shard_map/while/body/eval_jaxpr/ppermute | solution.py:19
  125.9 9.4 %collective-permute-start = (f32[36,12,128]{2,1,0:T(8,128)S(1)}, f32[36,12,128]{2,1,0:T(8,128)S(1)}, u32[]{:S(2)}, u32[]{:S(2)}) collective-permute-start(f32[36,12,128]{2,1,0:T(8,128)S(1)} %multiply_add_fusion.6), channel_id=1, source_target_pairs={{0,16},{16,32},{32,48},{48,64},{64,80},{80,96},{96,112},{112,128},... | collective-permute-start | bytes 663560 | tf_op jit(solution)/shard_map/while/body/eval_jaxpr/ppermute | solution.py:19
  129.7 10.1 %collective-permute-start.1 = (f32[36,12,128]{2,1,0:T(8,128)S(1)}, f32[36,12,128]{2,1,0:T(8,128)S(1)}, u32[]{:S(2)}, u32[]{:S(2)}) collective-permute-start(f32[36,12,128]{2,1,0:T(8,128)S(1)} %multiply_add_fusion.7), channel_id=1, source_target_pairs={{16,0},{32,16},{48,32},{64,48},{80,64},{96,80},{112,96},{128,112},... | collective-permute-start | bytes 663560 | tf_op jit(solution)/shard_map/while/body/eval_jaxpr/ppermute | solution.py:19
  139.8 10.2 %collective-permute-start = (f32[36,12,128]{2,1,0:T(8,128)S(1)}, f32[36,12,128]{2,1,0:T(8,128)S(1)}, u32[]{:S(2)}, u32[]{:S(2)}) collective-permute-start(f32[36,12,128]{2,1,0:T(8,128)S(1)} %multiply_add_fusion.6), channel_id=1, source_target_pairs={{0,16},{16,32},{32,48},{48,64},{64,80},{80,96},{96,112},{112,128},... | collective-permute-start | bytes 663560 | tf_op jit(solution)/shard_map/while/body/eval_jaxpr/ppermute | solution.py:19
  143.6 10.7 %collective-permute-start.1 = (f32[36,12,128]{2,1,0:T(8,128)S(1)}, f32[36,12,128]{2,1,0:T(8,128)S(1)}, u32[]{:S(2)}, u32[]{:S(2)}) collective-permute-start(f32[36,12,128]{2,1,0:T(8,128)S(1)} %multiply_add_fusion.7), channel_id=1, source_target_pairs={{16,0},{32,16},{48,32},{64,48},{80,64},{96,80},{112,96},{128,112},... | collective-permute-start | bytes 663560 | tf_op jit(solution)/shard_map/while/body/eval_jaxpr/ppermute | solution.py:19
  154.3 9.5 %collective-permute-start = (f32[36,12,128]{2,1,0:T(8,128)S(1)}, f32[36,12,128]{2,1,0:T(8,128)S(1)}, u32[]{:S(2)}, u32[]{:S(2)}) collective-permute-start(f32[36,12,128]{2,1,0:T(8,128)S(1)} %multiply_add_fusion.6), channel_id=1, source_target_pairs={{0,16},{16,32},{32,48},{48,64},{64,80},{80,96},{96,112},{112,128},... | collective-permute-start | bytes 663560 | tf_op jit(solution)/shard_map/while/body/eval_jaxpr/ppermute | solution.py:19
  158.3 9.5 %collective-permute-start.1 = (f32[36,12,128]{2,1,0:T(8,128)S(1)}, f32[36,12,128]{2,1,0:T(8,128)S(1)}, u32[]{:S(2)}, u32[]{:S(2)}) collective-permute-start(f32[36,12,128]{2,1,0:T(8,128)S(1)} %multiply_add_fusion.7), channel_id=1, source_target_pairs={{16,0},{32,16},{48,32},{64,48},{80,64},{96,80},{112,96},{128,112},... | collective-permute-start | bytes 663560 | tf_op jit(solution)/shard_map/while/body/eval_jaxpr/ppermute | solution.py:19
  167.8 9.9 %collective-permute-start = (f32[36,12,128]{2,1,0:T(8,128)S(1)}, f32[36,12,128]{2,1,0:T(8,128)S(1)}, u32[]{:S(2)}, u32[]{:S(2)}) collective-permute-start(f32[36,12,128]{2,1,0:T(8,128)S(1)} %multiply_add_fusion.6), channel_id=1, source_target_pairs={{0,16},{16,32},{32,48},{48,64},{64,80},{80,96},{96,112},{112,128},... | collective-permute-start | bytes 663560 | tf_op jit(solution)/shard_map/while/body/eval_jaxpr/ppermute | solution.py:19
  172.7 8.9 %collective-permute-start.1 = (f32[36,12,128]{2,1,0:T(8,128)S(1)}, f32[36,12,128]{2,1,0:T(8,128)S(1)}, u32[]{:S(2)}, u32[]{:S(2)}) collective-permute-start(f32[36,12,128]{2,1,0:T(8,128)S(1)} %multiply_add_fusion.7), channel_id=1, source_target_pairs={{16,0},{32,16},{48,32},{64,48},{80,64},{96,80},{112,96},{128,112},... | collective-permute-start | bytes 663560 | tf_op jit(solution)/shard_map/while/body/eval_jaxpr/ppermute | solution.py:19
  181.7 8.4 %collective-permute-start = (f32[36,12,128]{2,1,0:T(8,128)S(1)}, f32[36,12,128]{2,1,0:T(8,128)S(1)}, u32[]{:S(2)}, u32[]{:S(2)}) collective-permute-start(f32[36,12,128]{2,1,0:T(8,128)S(1)} %multiply_add_fusion.6), channel_id=1, source_target_pairs={{0,16},{16,32},{32,48},{48,64},{64,80},{80,96},{96,112},{112,128},... | collective-permute-start | bytes 663560 | tf_op jit(solution)/shard_map/while/body/eval_jaxpr/ppermute | solution.py:19
  186.0 8.0 %collective-permute-start.1 = (f32[36,12,128]{2,1,0:T(8,128)S(1)}, f32[36,12,128]{2,1,0:T(8,128)S(1)}, u32[]{:S(2)}, u32[]{:S(2)}) collective-permute-start(f32[36,12,128]{2,1,0:T(8,128)S(1)} %multiply_add_fusion.7), channel_id=1, source_target_pairs={{16,0},{32,16},{48,32},{64,48},{80,64},{96,80},{112,96},{128,112},... | collective-permute-start | bytes 663560 | tf_op jit(solution)/shard_map/while/body/eval_jaxpr/ppermute | solution.py:19
  194.1 8.0 %collective-permute-start = (f32[36,12,128]{2,1,0:T(8,128)S(1)}, f32[36,12,128]{2,1,0:T(8,128)S(1)}, u32[]{:S(2)}, u32[]{:S(2)}) collective-permute-start(f32[36,12,128]{2,1,0:T(8,128)S(1)} %multiply_add_fusion.6), channel_id=1, source_target_pairs={{0,16},{16,32},{32,48},{48,64},{64,80},{80,96},{96,112},{112,128},... | collective-permute-start | bytes 663560 | tf_op jit(solution)/shard_map/while/body/eval_jaxpr/ppermute | solution.py:19
  198.4 7.5 %collective-permute-start.1 = (f32[36,12,128]{2,1,0:T(8,128)S(1)}, f32[36,12,128]{2,1,0:T(8,128)S(1)}, u32[]{:S(2)}, u32[]{:S(2)}) collective-permute-start(f32[36,12,128]{2,1,0:T(8,128)S(1)} %multiply_add_fusion.7), channel_id=1, source_target_pairs={{16,0},{32,16},{48,32},{64,48},{80,64},{96,80},{112,96},{128,112},... | collective-permute-start | bytes 663560 | tf_op jit(solution)/shard_map/while/body/eval_jaxpr/ppermute | solution.py:19
  206.0 7.7 %collective-permute-start = (f32[36,12,128]{2,1,0:T(8,128)S(1)}, f32[36,12,128]{2,1,0:T(8,128)S(1)}, u32[]{:S(2)}, u32[]{:S(2)}) collective-permute-start(f32[36,12,128]{2,1,0:T(8,128)S(1)} %multiply_add_fusion.6), channel_id=1, source_target_pairs={{0,16},{16,32},{32,48},{48,64},{64,80},{80,96},{96,112},{112,128},... | collective-permute-start | bytes 663560 | tf_op jit(solution)/shard_map/while/body/eval_jaxpr/ppermute | solution.py:19
  210.1 7.5 %collective-permute-start.1 = (f32[36,12,128]{2,1,0:T(8,128)S(1)}, f32[36,12,128]{2,1,0:T(8,128)S(1)}, u32[]{:S(2)}, u32[]{:S(2)}) collective-permute-start(f32[36,12,128]{2,1,0:T(8,128)S(1)} %multiply_add_fusion.7), channel_id=1, source_target_pairs={{16,0},{32,16},{48,32},{64,48},{80,64},{96,80},{112,96},{128,112},... | collective-permute-start | bytes 663560 | tf_op jit(solution)/shard_map/while/body/eval_jaxpr/ppermute | solution.py:19
  217.6 8.0 %collective-permute-start = (f32[36,12,128]{2,1,0:T(8,128)S(1)}, f32[36,12,128]{2,1,0:T(8,128)S(1)}, u32[]{:S(2)}, u32[]{:S(2)}) collective-permute-start(f32[36,12,128]{2,1,0:T(8,128)S(1)} %multiply_add_fusion.6), channel_id=1, source_target_pairs={{0,16},{16,32},{32,48},{48,64},{64,80},{80,96},{96,112},{112,128},... | collective-permute-start | bytes 663560 | tf_op jit(solution)/shard_map/while/body/eval_jaxpr/ppermute | solution.py:19
  222.0 7.5 %collective-permute-start.1 = (f32[36,12,128]{2,1,0:T(8,128)S(1)}, f32[36,12,128]{2,1,0:T(8,128)S(1)}, u32[]{:S(2)}, u32[]{:S(2)}) collective-permute-start(f32[36,12,128]{2,1,0:T(8,128)S(1)} %multiply_add_fusion.7), channel_id=1, source_target_pairs={{16,0},{32,16},{48,32},{64,48},{80,64},{96,80},{112,96},{128,112},... | collective-permute-start | bytes 663560 | tf_op jit(solution)/shard_map/while/body/eval_jaxpr/ppermute | solution.py:19
  229.5 1.0 copy-start.1
  229.5 1.1 copy-start.2
  232.6 45.0 %copy-start.3 = (f32[25,256]{1,0:T(8,128)S(1)}, f32[25,256]{1,0:T(8,128)}, u32[]{:S(2)}) copy-start(f32[25,256]{1,0:T(8,128)} %param.15) | copy-start | bytes 76804
  277.6 5.1 %copy-start.4 = (f32[25,256]{1,0:T(8,128)S(1)}, f32[25,256]{1,0:T(8,128)}, u32[]{:S(2)}) copy-start(f32[25,256]{1,0:T(8,128)} %param.13) | copy-start | bytes 76804
  277.6 5.1 %copy-start.5 = (f32[25,256]{1,0:T(8,128)S(1)}, f32[25,256]{1,0:T(8,128)}, u32[]{:S(2)}) copy-start(f32[25,256]{1,0:T(8,128)} %param.14) | copy-start | bytes 76804
  277.7 5.1 %collective-permute-start.2 = (f32[5,1,128]{2,1,0:T(1,128)S(1)}, f32[5,1,128]{2,1,0:T(1,128)S(1)}, u32[]{:S(2)}, u32[]{:S(2)}) collective-permute-start(f32[5,1,128]{2,1,0:T(1,128)S(1)} %get-tuple-element.101), channel_id=1, source_target_pairs={{0,16},{16,32},{32,48},{48,64},{64,80},{80,96},{96,112},{112,128},... | collective-permute-start | bytes 7688 | tf_op jit(solution)/shard_map/ppermute | solution.py:29
  281.4 4.6 %collective-permute-start.3 = (f32[5,1,128]{2,1,0:T(1,128)S(1)}, f32[5,1,128]{2,1,0:T(1,128)S(1)}, u32[]{:S(2)}, u32[]{:S(2)}) collective-permute-start(f32[5,1,128]{2,1,0:T(1,128)S(1)} %get-tuple-element.102), channel_id=1, source_target_pairs={{16,0},{32,16},{48,32},{64,48},{80,64},{96,80},{112,96},{128,112},... | collective-permute-start | bytes 7688 | tf_op jit(solution)/shard_map/ppermute | solution.py:30
  286.1 5.1 %collective-permute-start.4 = (f32[5,1,128]{2,1,0:T(1,128)S(1)}, f32[5,1,128]{2,1,0:T(1,128)S(1)}, u32[]{:S(2)}, u32[]{:S(2)}) collective-permute-start(f32[5,1,128]{2,1,0:T(1,128)S(1)} %get-tuple-element.97), channel_id=1, source_target_pairs={{0,16},{16,32},{32,48},{48,64},{64,80},{80,96},{96,112},{112,128},... | collective-permute-start | bytes 7688 | tf_op jit(solution)/shard_map/ppermute | solution.py:29
  289.9 4.3 collective-permute-start.5
  294.3 5.3 %collective-permute-start.6 = (f32[5,1,128]{2,1,0:T(1,128)S(1)}, f32[5,1,128]{2,1,0:T(1,128)S(1)}, u32[]{:S(2)}, u32[]{:S(2)}) collective-permute-start(f32[5,1,128]{2,1,0:T(1,128)S(1)} %get-tuple-element.93), channel_id=1, source_target_pairs={{0,16},{16,32},{32,48},{48,64},{64,80},{80,96},{96,112},{112,128},... | collective-permute-start | bytes 7688 | tf_op jit(solution)/shard_map/ppermute | solution.py:29
  298.4 4.3 collective-permute-start.7
  302.8 5.3 %collective-permute-start.8 = (f32[5,1,128]{2,1,0:T(1,128)S(1)}, f32[5,1,128]{2,1,0:T(1,128)S(1)}, u32[]{:S(2)}, u32[]{:S(2)}) collective-permute-start(f32[5,1,128]{2,1,0:T(1,128)S(1)} %get-tuple-element.89), channel_id=1, source_target_pairs={{0,16},{16,32},{32,48},{48,64},{64,80},{80,96},{96,112},{112,128},... | collective-permute-start | bytes 7688 | tf_op jit(solution)/shard_map/ppermute | solution.py:29
  306.9 4.3 collective-permute-start.9
